TPU v7x, 512 devices: a whole 4x8x8 slice. The times are simulated.
512 devices in a mesh: ctx: 64 (over y, z_lo, core), dp: 8 (over z_hi, x).
Axes of the slice: x: 4, y: 8, z: 8 (z_hi: 2, z_lo: 4; z = z_hi * 4 + z_lo), core: 2. Of those that a mesh axis runs over, the one named last changes fastest.
Arguments:
- features: bfloat16 [8, 12288, 1536], P('dp', 'ctx'), may hold values from -6 to 6
- bottleneck: bfloat16 [8, 12288, 384], P('dp', 'ctx'), may hold values from -6 to 6
- node_noise: bfloat16 [8, 12288, 1536], P('dp', 'ctx'), may hold values from -6 to 6
- targets: bfloat16 [8, 12288, 1536], P('dp', 'ctx'), may hold values from -15 to 15
- entry_weight: bfloat16 [384, 1536], P('ctx'), may hold values from -0.3125 to 0.3125
- conv_filters: bfloat16 [3, 1536, 384], P(None, None, 'ctx'), may hold values from -0.09375 to 0.09375
- exit_weight: bfloat16 [384, 1536], P('ctx'), may hold values from -0.3125 to 0.3125
Outputs:
- blended: bfloat16 [8, 12288, 1536], P('dp', 'ctx')
- estimate: float32 [384, 1536], P('ctx')
All inputs are finite; a program needn't handle non-finite values.
Results may differ from a plain program's by a relative error of at most 0.015.
The roundings to bfloat16 on the way count: a program that leaves them out, or rounds other values in their place, can miss the bound.
Values may be sent and summed in bfloat16 or wider, within the bound.
No kernel may reach another device: no remote copies, remote signals or barrier semaphores. Data moves between devices by JAX's collectives and lax.ppermute only.
A program may use at most 64 MiB of HBM per device.

v0:
```python
import jax
import jax.numpy as jnp
from jax import lax
from jax.sharding import Mesh
from jax.sharding import PartitionSpec as P

DILATION = 32
NOISE_SCALE = 0.1
CTX = ("y", "zl", "c")
DP = ("zh", "x")


def _size(axes):
    n = 1
    for a in axes:
        n *= lax.axis_size(a)
    return n


def body(features, bottleneck, node_noise, targets, entry_weight, conv_filters, exit_weight):
    feats = features[0]
    bottle = bottleneck[0]
    jitter = node_noise[0]
    goal = targets[0].astype(jnp.float32)
    rows, chans = feats.shape
    bot = bottle.shape[1]
    n_ctx = _size(CTX)
    ny, nz, nc = (lax.axis_size(a) for a in CTX)
    shard = entry_weight.shape[0]
    bottle_perm = (
        bottle.reshape(rows, ny, nz, nc, shard).transpose(0, 3, 2, 1, 4).reshape(rows, bot)
    )
    summed = lax.dot_general(
        bottle_perm, jitter, (((0,), (0,)), ((), ())), preferred_element_type=jnp.float32
    )
    for axis in ("c", "zl", "y"):
        summed = lax.psum_scatter(summed, axis, scatter_dimension=0, tiled=True)
    summed_all = lax.all_gather(summed, DP, axis=0, tiled=False)
    n_dp = _size(DP)
    me_dp = lax.axis_index("zh") * lax.axis_size("x") + lax.axis_index("x")
    conv_rows = conv_filters.transpose(2, 0, 1).reshape(shard, -1)
    parts = [
        lax.dynamic_slice_in_dim(w.reshape(shard, n_dp, -1), me_dp, 1, axis=1)[:, 0]
        for w in (entry_weight, conv_rows, exit_weight)
    ]
    piece = jnp.concatenate(parts, axis=1)
    packed = lax.all_gather(piece, CTX + DP, axis=0, tiled=False)
    packed = packed.reshape(n_ctx, n_dp, shard, -1)
    cw = chans // n_dp
    w_entry = packed[..., :cw].transpose(0, 2, 1, 3).reshape(n_ctx * shard, chans)
    w_conv = packed[..., cw : 4 * cw].transpose(0, 2, 1, 3).reshape(bot, 3, chans)
    w_exit = packed[..., 4 * cw :].transpose(0, 2, 1, 3).reshape(n_ctx * shard, chans)
    spacing = DILATION
    edge_in = jnp.concatenate([feats, bottle, jitter], axis=1)
    pairs_up = [(i, i + 1) for i in range(n_ctx - 1)]
    pairs_down = [(i + 1, i) for i in range(n_ctx - 1)]
    from_prev = lax.ppermute(edge_in[rows - spacing :], CTX, pairs_up)
    from_next = lax.ppermute(edge_in[:spacing], CTX, pairs_down)
    ext = jnp.concatenate([from_prev, edge_in, from_next], axis=0)
    ext_feats = ext[:, :chans]
    ext_bottle = ext[:, chans : chans + bot]
    ext_jitter = ext[:, chans + bot :]
    baseline = ext_feats.astype(jnp.float32) + jnp.dot(
        ext_bottle, w_entry, preferred_element_type=jnp.float32
    )
    offset = ext_jitter.astype(jnp.float32) * NOISE_SCALE
    state = jnp.stack([baseline + offset, baseline - offset])
    activated = jax.nn.gelu(state).astype(jnp.bfloat16)
    mixed = None
    for k in range(3):
        term = lax.dot_general(
            activated[:, k * spacing : k * spacing + rows],
            w_conv[:, k, :],
            (((2,), (1,)), ((), ())),
            preferred_element_type=jnp.float32,
        )
        mixed = term if mixed is None else mixed + term
    inner = jax.nn.gelu(mixed).astype(jnp.bfloat16)
    outs = state[:, spacing : spacing + rows] + jnp.dot(
        inner, w_exit, preferred_element_type=jnp.float32
    )
    upper = outs[0]
    lower = outs[1]
    blended = ((upper + lower) * 0.5).astype(jnp.bfloat16)[None]
    local_gap = jnp.sum((upper - lower) * (upper + lower - 2.0 * goal)) / (rows * n_ctx * chans)
    slots = jnp.zeros((n_dp,), jnp.float32).at[me_dp].set(local_gap)
    gaps = lax.psum(slots, CTX + DP)
    factors = gaps / (2.0 * NOISE_SCALE)
    estimate = jnp.sum(factors[:, None, None] * summed_all, axis=0)
    return (blended, estimate)


def solution(mesh):
    ctx_n, dp_n = mesh.devices.shape
    devices = mesh.devices.reshape(8, ctx_n // 16, 2, dp_n // 4, 4)
    fine = Mesh(devices, CTX + DP)
    return jax.shard_map(
        body,
        mesh=fine,
        in_specs=(
            P(DP, CTX, None),
            P(DP, CTX, None),
            P(DP, CTX, None),
            P(DP, CTX, None),
            P(CTX, None),
            P(None, None, CTX),
            P(CTX, None),
        ),
        out_specs=(P(DP, CTX, None), P(CTX, None)),
        check_vma=False,
    )
```

profile of v0, /device:TPU:1, one launch (start us, length us, event | category | flops | bytes accessed | tf_op | source)
XLA Modules:
  0.0 1673.8 jit_solution(16459171354127405826)
XLA Ops:
  9.4 1.9 fusion.43
  11.4 25.1 %reduce-scatter.5.cloned.1.call-done = f32[192,1536]{1,0:T(8,128)} async-done(((f32[384,1536]{1,0:T(8,128)}), f32[192,1536]{1,0:T(8,128)}) %reduce-scatter.5.cloned.1.call-update) | async-done | bytes 1179664 | tf_op jit(solution)/shard_map/reduce_scatter | solution.py:37
  37.8 1.9 collective-permute-start.1
  39.7 3.6 collective-permute-start
  45.3 32.1 %reduce-scatter.7.cloned.1.call-done = f32[48,1536]{1,0:T(8,128)} async-done(((f32[192,1536]{1,0:T(8,128)}), f32[48,1536]{1,0:T(8,128)}) %reduce-scatter.7.cloned.1.call-update) | async-done | bytes 294928 | tf_op jit(solution)/shard_map/reduce_scatter | solution.py:37
  77.4 17.1 %fusion = f32[8,1536]{1,0:T(8,128)S(1)} fusion(f32[48,1536]{1,0:T(8,128)} %reduce-scatter.7.cloned.1.call-done), kind=kCustom, calls=%all-reduce-scatter | all-reduce-scatter fusion | flops 98305 | bytes 346112
  94.6 2.1 collective-permute-start.2
  96.7 3.5 collective-permute-start.3
  100.2 1.4 pad_maximum_fusion.1
  101.9 1356.0 %all-gather.6.cloned.1.call-done = bf16[512,6,960]{2,1,0:T(8,128)(2,1)} async-done(((bf16[1,6,960]{2,1,0:T(8,128)(2,1)}), bf16[512,6,960]{2,1,0:T(8,128)(2,1)}) %all-gather.6.cloned.1.call-update) | async-done | bytes 5898256 | tf_op jit(solution)/shard_map/all_gather | solution.py:47
  1457.9 6.9 copy.60
  1465.1 4.1 slice_bitcast_fusion
  1469.2 1.3 copy.35
  1470.4 3.8 reshape.88
  1475.5 3.8 reshape.71
  1479.2 4.4 copy.31
  1483.6 12.4 reshape.72
  1496.0 12.1 fusion.49
  1508.1 1.8 subtract_bitcast_fusion
  1512.3 1.6 convolution_add_fusion.2
  1513.9 5.6 convolution_add_fusion
  1519.5 3.4 multiply_reduce_fusion
  1523.6 37.9 %all-gather.3 = f32[8,6,1536]{2,1,0:T(8,128)S(1)} all-gather(f32[1,6,1536]{2,1,0:T(8,128)S(1)} %dynamic-slice_bitcast_fusion), channel_id=3, replica_groups=mesh['y'=8,'zl'=4,'c'=2,'zh'=2,'x'=4] {'zh','x'}, dimensions={0}, use_global_device_ids=true | all-gather | bytes 331776 | tf_op jit(solution)/shard_map/all_gather | solution.py:38
  1561.5 104.2 %psum.7 = f32[8]{0:T(128)S(1)} all-reduce(f32[8]{0:T(128)S(1)} %scatter.4), channel_id=1, replica_groups=mesh['y'=8,'zl'=4,'c'=2,'zh'=2,'x'=4] {'y','zl','c','zh','x'}, use_global_device_ids=true, to_apply=%region_1.0 | all-reduce | flops 8 | bytes 64 | tf_op jit(solution)/shard_map/psum | solution.py:87
  (59 shorter events, 9.0 us)
Async XLA Ops:
  8.0 1.4 copy-start
  8.0 28.4 %reduce-scatter.5.cloned.1.call-start = ((), (), s32[]{:S(2)}) async-start(), calls=%async_computation.2 | async-start | bytes 3538944 | tf_op jit(solution)/shard_map/reduce_scatter | solution.py:37
  11.3 25.2 %copy-start.9 = (bf16[6,1536]{1,0:T(8,128)(2,1)S(1)}, bf16[6,1536]{1,0:T(8,128)(2,1)}, u32[]{:S(2)}) copy-start(bf16[6,1536]{1,0:T(8,128)(2,1)} %param.15) | copy-start | bytes 55300
  11.3 25.3 %copy-start.10 = (bf16[6,1536]{1,0:T(8,128)(2,1)S(1)}, bf16[6,1536]{1,0:T(8,128)(2,1)}, u32[]{:S(2)}) copy-start(bf16[6,1536]{1,0:T(8,128)(2,1)} %param.13) | copy-start | bytes 55300
  11.3 25.5 %copy-start.8 = (bf16[3,1536,6]{1,2,0:T(8,128)(2,1)S(1)}, bf16[3,1536,6]{1,2,0:T(8,128)(2,1)}, u32[]{:S(2)}) copy-start(bf16[3,1536,6]{1,2,0:T(8,128)(2,1)} %param.14) | copy-start | bytes 165892
  11.3 26.4 %copy-start.1 = (bf16[1,192,1536]{2,1,0:T(8,128)(2,1)S(1)}, bf16[1,192,1536]{2,1,0:T(8,128)(2,1)}, u32[]{:S(2)}) copy-start(bf16[1,192,1536]{2,1,0:T(8,128)(2,1)} %param.9) | copy-start | bytes 1769476
  11.3 26.4 %copy-start.4 = (bf16[1,192,384]{2,1,0:T(8,128)(2,1)S(1)}, bf16[1,192,384]{2,1,0:T(8,128)(2,1)}, u32[]{:S(2)}) copy-start(bf16[1,192,384]{2,1,0:T(8,128)(2,1)} %param.10) | copy-start | bytes 442372
  11.3 66.1 %reduce-scatter.7.cloned.1.call-start = ((), (), s32[]{:S(2)}) async-start(), calls=%async_computation.3 | async-start | bytes 1474560 | tf_op jit(solution)/shard_map/reduce_scatter | solution.py:37
  36.5 1421.4 %all-gather.6.cloned.1.call-start = ((), (), s32[]{:S(2)}) async-start(), calls=%async_computation.4 | async-start | bytes 8404992 | tf_op jit(solution)/shard_map/all_gather | solution.py:47
  37.8 62.4 %collective-permute-start.1 = (bf16[32,3456]{1,0:T(8,128)(2,1)S(1)}, bf16[32,3456]{1,0:T(8,128)(2,1)S(1)}, u32[]{:S(2)}, u32[]{:S(2)}) collective-permute-start(bf16[32,3456]{1,0:T(8,128)(2,1)S(1)} %get-tuple-element.24), channel_id=1, source_target_pairs={{8,0},{16,8},{24,16},{32,24},{40,32},{48,40},{56,48},{64,56},{72,6... | collective-permute-start | bytes 663560 | tf_op jit(solution)/shard_map/ppermute | solution.py:58
  39.7 60.5 %collective-permute-start = (bf16[32,3456]{1,0:T(8,128)(2,1)S(1)}, bf16[32,3456]{1,0:T(8,128)(2,1)S(1)}, u32[]{:S(2)}, u32[]{:S(2)}) collective-permute-start(bf16[32,3456]{1,0:T(8,128)(2,1)S(1)} %get-tuple-element.23), channel_id=1, source_target_pairs={{0,8},{8,16},{16,24},{24,32},{32,40},{40,48},{48,56},{56,64},{64,7... | collective-permute-start | bytes 663560 | tf_op jit(solution)/shard_map/ppermute | solution.py:57
  94.6 7.0 collective-permute-start.2
  96.7 4.9 collective-permute-start.3
  1496.0 12.1 copy-start.3
  1509.9 1.1 copy-start.2
  1511.0 1.2 copy-start.5
  1512.3 1.6 copy-start.6
  1513.9 5.6 copy-start.7
Sparse Core Ops, SparseCore 0:
  11.6 24.7 reduce-scatter.4
  39.5 37.8 reduce-scatter.6
Sparse Core Ops, SparseCore 1:
  39.7 1418.1 all-gather.5
where the time goes:
time: 1670 us
  waiting for transfers between devices  1410 us (84%)
  blocking collectives  159 us (10%)
  local copies, waits for them, and re-layouts  54.3 us (3%)
  between operations  17.1 us (1%)
    all_gather x1, waiting for transfers between devices, body(): packed = lax.all_gather(piece, CTX + DP, axis=0, tiled=False)  1360 us
    psum x1, blocking collectives, body(): gaps = lax.psum(slots, CTX + DP)  104 us
    reduce_scatter x2, waiting for transfers between devices, body(): summed = lax.psum_scatter(summed, axis, scatter_dimension=0, tiled=True)  57.2 us
    all_gather x1, blocking collectives, body(): summed_all = lax.all_gather(summed, DP, axis=0, tiled=False)  37.9 us
  transfers between devices with their start and end apart: 7, of which 3 were waited for; matrix products, arithmetic and copies ran while one was open for 1% of the time, Pallas kernels for 0%

commit v1 on v0

--- a/solution.py
+++ b/solution.py
@@ -84,7 +84,7 @@
     blended = ((upper + lower) * 0.5).astype(jnp.bfloat16)[None]
     local_gap = jnp.sum((upper - lower) * (upper + lower - 2.0 * goal)) / (rows * n_ctx * chans)
     slots = jnp.zeros((n_dp,), jnp.float32).at[me_dp].set(local_gap)
-    gaps = lax.psum(slots, CTX + DP)
+    gaps = jnp.sum(lax.all_gather(slots, CTX + DP), axis=0)
     factors = gaps / (2.0 * NOISE_SCALE)
     estimate = jnp.sum(factors[:, None, None] * summed_all, axis=0)
     return (blended, estimate)

time: 1670 us -> 2950 us (1.77)
  blocking collectives: 159 us -> 1470 us
  waiting for transfers between devices: 1410 us -> 1370 us
    all_gather x0 -> x1, blocking collectives: none -> 1410 us  [body(): gaps = jnp.sum(lax.all_gather(slots, CTX + DP), axis=0)]
    psum x1 -> x0, blocking collectives: 104 us -> none  [body(): gaps = lax.psum(slots, CTX + DP)]
    all_gather x1, waiting for transfers between devices: 1360 us -> 1320 us  [body(): packed = lax.all_gather(piece, CTX + DP, axis=0, tiled=False)]
where the time goes in v1:
time: 2950 us
  blocking collectives  1470 us (50%)
  waiting for transfers between devices  1370 us (46%)
  local copies, waits for them, and re-layouts  53.9 us (2%)
    all_gather x1, blocking collectives, body(): gaps = jnp.sum(lax.all_gather(slots, CTX + DP), axis=0)  1410 us
    all_gather x1, waiting for transfers between devices, body(): packed = lax.all_gather(piece, CTX + DP, axis=0, tiled=False)  1320 us
  transfers between devices with their start and end apart: 7, of which 3 were waited for; matrix products, arithmetic and copies ran while one was open for 1% of the time, Pallas kernels for 0%

profile of v1, /device:TPU:1, one launch (start us, length us, event | category | flops | bytes accessed | tf_op | source)
XLA Modules:
  0.0 2945.7 jit_solution(18153754981604052314)
XLA Ops:
  9.4 1.9 fusion.43
  11.4 25.1 reduce-scatter.5.cloned.1.call-done
  37.8 1.9 collective-permute-start.1
  39.7 3.6 collective-permute-start
  45.3 32.1 %reduce-scatter.7.cloned.1.call-done = f32[48,1536]{1,0:T(8,128)} async-done(((f32[192,1536]{1,0:T(8,128)}), f32[48,1536]{1,0:T(8,128)}) %reduce-scatter.7.cloned.1.call-update) | async-done | bytes 294928 | tf_op jit(solution)/shard_map/reduce_scatter | solution.py:37
  77.4 17.1 fusion
  94.6 2.1 collective-permute-start.2
  96.7 3.5 collective-permute-start.3
  100.2 1.4 pad_maximum_fusion.1
  101.9 39.9 %all-gather.4 = f32[8,6,1536]{2,1,0:T(8,128)} all-gather(f32[1,6,1536]{2,1,0:T(8,128)S(1)} %dynamic-slice_bitcast_fusion), channel_id=3, replica_groups=mesh['y'=8,'zl'=4,'c'=2,'zh'=2,'x'=4] {'zh','x'}, dimensions={0}, use_global_device_ids=true | all-gather | bytes 331776 | tf_op jit(solution)/shard_map/all_gather | solution.py:38
  141.8 1316.1 %all-gather.7.cloned.1.call-done = bf16[512,6,960]{2,1,0:T(8,128)(2,1)} async-done(((bf16[1,6,960]{2,1,0:T(8,128)(2,1)}), bf16[512,6,960]{2,1,0:T(8,128)(2,1)}) %all-gather.7.cloned.1.call-update) | async-done | bytes 5898256 | tf_op jit(solution)/shard_map/all_gather | solution.py:47
  1457.9 6.9 copy.60
  1465.1 4.1 slice_bitcast_fusion
  1470.4 3.7 reshape.95
  1474.2 1.3 copy.30
  1475.5 3.8 reshape.74
  1479.2 4.4 copy.31
  1483.6 12.4 reshape.75
  1496.0 11.9 fusion.49
  1507.9 1.8 subtract_bitcast_fusion
  1512.0 1.6 convolution_add_fusion.2
  1513.6 5.6 convolution_add_fusion
  1519.2 3.4 multiply_reduce_fusion
  1523.3 1413.7 %all-gather.3 = f32[512,1,8]{2,1,0:T(1,128)S(1)} all-gather(f32[1,1,8]{2,1,0:T(1,128)S(1)} %scatter.6), channel_id=1, replica_groups=mesh['y'=8,'zl'=4,'c'=2,'zh'=2,'x'=4] {'y','zl','c','zh','x'}, dimensions={0}, use_global_device_ids=true | all-gather | bytes 16416 | tf_op jit(solution)/shard_map/all_gather | solution.py:87
  (62 shorter events, 9.5 us)
Async XLA Ops:
  8.0 1.4 copy-start
  8.0 28.4 reduce-scatter.5.cloned.1.call-start
  11.3 25.2 copy-start.10
  11.3 25.3 copy-start.11
  11.3 25.5 copy-start.9
  11.3 26.4 copy-start.1
  11.3 26.4 copy-start.4
  11.3 66.1 %reduce-scatter.7.cloned.1.call-start = ((), (), s32[]{:S(2)}) async-start(), calls=%async_computation.3 | async-start | bytes 1474560 | tf_op jit(solution)/shard_map/reduce_scatter | solution.py:37
  36.5 1421.4 %all-gather.7.cloned.1.call-start = ((), (), s32[]{:S(2)}) async-start(), calls=%async_computation.4 | async-start | bytes 8404992 | tf_op jit(solution)/shard_map/all_gather | solution.py:47
  37.8 62.4 %collective-permute-start.1 = (bf16[32,3456]{1,0:T(8,128)(2,1)S(1)}, bf16[32,3456]{1,0:T(8,128)(2,1)S(1)}, u32[]{:S(2)}, u32[]{:S(2)}) collective-permute-start(bf16[32,3456]{1,0:T(8,128)(2,1)S(1)} %get-tuple-element.24), channel_id=1, source_target_pairs={{8,0},{16,8},{24,16},{32,24},{40,32},{48,40},{56,48},{64,56},{72,6... | collective-permute-start | bytes 663560 | tf_op jit(solution)/shard_map/ppermute | solution.py:58
  39.7 60.5 %collective-permute-start = (bf16[32,3456]{1,0:T(8,128)(2,1)S(1)}, bf16[32,3456]{1,0:T(8,128)(2,1)S(1)}, u32[]{:S(2)}, u32[]{:S(2)}) collective-permute-start(bf16[32,3456]{1,0:T(8,128)(2,1)S(1)} %get-tuple-element.23), channel_id=1, source_target_pairs={{0,8},{8,16},{16,24},{24,32},{32,40},{40,48},{48,56},{56,64},{64,7... | collective-permute-start | bytes 663560 | tf_op jit(solution)/shard_map/ppermute | solution.py:57
  94.6 7.0 collective-permute-start.2
  96.7 4.9 collective-permute-start.3
  1496.0 11.9 copy-start.3
  1509.6 1.1 copy-start.2
  1510.8 1.2 copy-start.6
  1512.0 1.6 copy-start.7
  1513.6 5.6 copy-start.8
  1519.2 1418.4 %copy-start.5 = (f32[8,6,1536]{2,1,0:T(8,128)S(1)}, f32[8,6,1536]{2,1,0:T(8,128)}, u32[]{:S(2)}) copy-start(f32[8,6,1536]{2,1,0:T(8,128)} %all-gather.4) | copy-start | bytes 884740
Sparse Core Ops, SparseCore 0:
  11.6 24.7 reduce-scatter.4
  39.5 37.8 reduce-scatter.6
Sparse Core Ops, SparseCore 1:
  39.7 1418.1 all-gather.6
